TPU v7x, 128 devices: a whole 4x4x4 slice. The times are simulated.
128 devices in a mesh: tm: 32 (over x, z, core), chan: 4 (over y).
Axes of the slice: x: 4, y: 4, z: 4, core: 2. Of those that a mesh axis runs over, the one named last changes fastest.
Arguments:
- inputs: bfloat16 [64, 256, 512], P('tm'), may hold values from -6 to 6
- decay: float32 [64, 512], P('tm', 'chan'), may hold values from 0 to 1, as said below
- kernel_b: bfloat16 [9, 512, 256], P(None, 'chan'), may hold values from -0.125 to 0.125
- kernel_c: bfloat16 [9, 256, 512], P(None, 'chan'), may hold values from -0.09375 to 0.09375
- cotangent: bfloat16 [64, 256, 512], P('tm', 'chan'), may hold values from -0.03125 to 0.03125
Outputs:
- grad_b: float32 [9, 512, 256], P(None, 'chan')
- grad_c: float32 [9, 256, 512], P(None, 'chan')
- decay_grad: float32 [64, 512], P('tm', 'chan')
Inputs may be any that keep to these rules, and one draw needn't show every extreme that they name: decay lies strictly between 0 and 1.
All inputs are finite; a program needn't handle non-finite values.
Results may differ from a plain program's by a relative error of at most 0.003.
Values may be sent and summed in bfloat16 or wider, within the bound.
No kernel may reach another device: no remote copies, remote signals or barrier semaphores. Data moves between devices by JAX's collectives and lax.ppermute only.
A program may use at most 128 MiB of HBM per device.

v0:
```python
import jax
import jax.numpy as jnp
from jax import lax
from jax.sharding import PartitionSpec as P

W = 64
offsets = ((-1, -1), (-1, 0), (-1, 1), (0, -1), (0, 0), (0, 1), (1, -1), (1, 0), (1, 1))


def passed_along(value, axis, steps):
    count = lax.axis_size(axis)
    first, last = (max(0, -steps), min(count, count - steps))
    return lax.ppermute(value, axis, [(source, source + steps) for source in range(first, last)])


def shift_cells(source, row_shift, col_shift, grid_width):
    cell_count = source.shape[-1]
    margin = grid_width + 1
    padded = jnp.pad(source, [(0, 0)] * (source.ndim - 1) + [(margin, margin)])
    first_cell = margin + row_shift * grid_width + col_shift
    shifted = lax.slice_in_dim(padded, first_cell, first_cell + cell_count, axis=source.ndim - 1)
    column = jnp.arange(cell_count) % grid_width
    inside = (column + col_shift >= 0) & (column + col_shift < grid_width)
    return jnp.where(inside, shifted, jnp.zeros((), source.dtype))


def stencil_stack(source, grid_width, decay_factor):
    parts = [
        shift_cells(source, decay_factor * pair[0], decay_factor * pair[1], grid_width)
        for pair in offsets
    ]
    return jnp.stack(parts, axis=source.ndim - 2)


def body(inputs, decay, kernel_b, kernel_c, cotangent):
    local_rows = kernel_b.shape[1]
    cell_count = inputs.shape[-1]
    blank_state = jnp.zeros((local_rows, cell_count), jnp.float32)
    input_stack = stencil_stack(inputs, W, 1)
    drives = jnp.einsum("kpc,fkcs->fps", kernel_b, input_stack, preferred_element_type=jnp.float32)

    def advance(current, frame_pair):
        frame_rate, drive = frame_pair
        current = frame_rate[:, None] * current + drive
        return (current, current)

    local_end, local_states = lax.scan(advance, blank_state, (decay, drives))
    decay_total = jnp.prod(decay, axis=0)

    def relay_state(turn_index, carried):
        outgoing = decay_total[:, None] * carried + local_end
        return passed_along(outgoing, "tm", 1)

    entering = lax.fori_loop(0, lax.axis_size("tm") - 1, relay_state, blank_state)
    cumulative = jnp.cumprod(decay, axis=0)
    states = local_states + cumulative[:, :, None] * entering[None]
    previous = jnp.concatenate([entering[None], states[:-1]], axis=0)
    states_bf = states.astype(jnp.bfloat16)
    cot_stack = stencil_stack(cotangent, W, -1)
    injected = lax.psum_scatter(
        jnp.einsum("kup,fkus->pfs", kernel_c, cot_stack, preferred_element_type=jnp.float32),
        "chan",
        scatter_dimension=0,
        tiled=True,
    )
    injected = jnp.moveaxis(injected, 1, 0)

    def retreat(carried, frame_pair):
        frame_rate, source = frame_pair
        adjoint = source + carried
        return (frame_rate[:, None] * adjoint, adjoint)

    message, local_adjoint = lax.scan(retreat, blank_state, (decay, injected), reverse=True)

    def relay_adjoint(turn_index, carried):
        outgoing = decay_total[:, None] * carried + message
        return passed_along(outgoing, "tm", -1)

    arriving = lax.fori_loop(0, lax.axis_size("tm") - 1, relay_adjoint, blank_state)
    suffix = jnp.flip(jnp.cumprod(jnp.flip(decay, 0), 0), 0)
    later_decay = jnp.concatenate([suffix[1:], jnp.ones_like(decay[:1])], axis=0)
    adjoint = local_adjoint + later_decay[:, :, None] * arriving[None]
    decay_grad = jnp.sum(adjoint * previous, axis=2)
    adjoint_bf = adjoint.astype(jnp.bfloat16)
    grad_b_part = jnp.einsum(
        "fps,fkcs->kpc", adjoint_bf, input_stack, preferred_element_type=jnp.float32
    )
    shifted = stencil_stack(lax.all_gather(states_bf, "chan", axis=1, tiled=True), W, 1)
    grad_c_part = jnp.einsum(
        "fus,fkps->kup", cotangent, shifted, preferred_element_type=jnp.float32
    )
    grad_b, grad_c = lax.psum((grad_b_part, grad_c_part), "tm")
    return (grad_b, grad_c, decay_grad)


def solution(mesh):
    in_specs = (
        P("tm", None, None),
        P("tm", "chan"),
        P(None, "chan", None),
        P(None, "chan", None),
        P("tm", "chan", None),
    )
    out_specs = (P(None, "chan", None), P(None, "chan", None), P("tm", "chan"))
    return jax.shard_map(body, mesh=mesh, in_specs=in_specs, out_specs=out_specs, check_vma=False)
```

profile of v0, /device:TPU:1, one launch (start us, length us, event | category | flops | bytes accessed | tf_op | source)
XLA Modules:
  0.0 817.5 jit_solution(8985757919530302460)
XLA Ops:
  20.7 275.2 %while.51 = (s32[]{:T(128)}, f32[128,512]{1,0:T(8,128)S(1)}, f32[128]{0:T(128)S(1)}, f32[128,512]{1,0:T(8,128)S(1)}, s32[]{:T(128)}) while((s32[]{:T(128)}, f32[128,512]{1,0:T(8,128)S(1)}, f32[128]{0:T(128)S(1)}, f32[128,512]{1,0:T(8,128)S(1)}, s32[]{:T(128)}) %tuple.101), condition=%wide.region_12.13_spmd, body=%wide.region_11.12_spmd.sunk | while | flops 131074 | bytes 1835621 | solution.py:54
  147.5 6.5 collective-permute-start.1
  157.4 6.5 collective-permute-start.1
  167.3 6.5 collective-permute-start.1
  177.2 6.5 collective-permute-start.1
  187.1 6.5 collective-permute-start.1
  197.0 6.5 collective-permute-start.1
  206.9 6.5 collective-permute-start.1
  216.8 6.5 collective-permute-start.1
  226.7 6.5 collective-permute-start.1
  300.5 49.7 %all-gather.2.cloned.1.call-done = bf16[2,512,512]{2,1,0:T(8,128)(2,1)} async-done(((bf16[2,128,512]{2,1,0:T(8,128)(2,1)}), bf16[2,512,512]{2,1,0:T(8,128)(2,1)}) %all-gather.2.cloned.1.call-update) | async-done | bytes 1048592 | tf_op jit(solution)/shard_map/all_gather | solution.py:88
  361.1 23.6 %reduce-scatter.2.cloned.1.call-done = f32[128,2,512]{0,2,1:T(8,128)} async-done(((f32[512,2,512]{0,2,1:T(8,128)}), f32[128,2,512]{0,2,1:T(8,128)}) %reduce-scatter.2.cloned.1.call-update) | async-done | bytes 524304 | tf_op jit(solution)/shard_map/reduce_scatter | solution.py:60
  387.4 279.4 %while.50 = (s32[]{:T(128)}, f32[128,512]{1,0:T(8,128)S(1)}, f32[128]{0:T(128)S(1)}, f32[128,512]{1,0:T(8,128)S(1)}, s32[]{:T(128)}) while((s32[]{:T(128)}, f32[128,512]{1,0:T(8,128)S(1)}, f32[128]{0:T(128)S(1)}, f32[128,512]{1,0:T(8,128)S(1)}, s32[]{:T(128)}) %tuple.113), condition=%wide.region_6.7_spmd, body=%wide.region_5.6_spmd.sunk | while | flops 131074 | bytes 1835621 | solution.py:79
  490.8 7.7 collective-permute-done
  500.6 7.9 collective-permute-done
  510.5 7.9 collective-permute-done
  520.4 7.9 collective-permute-done
  530.3 7.9 collective-permute-done
  540.2 7.9 collective-permute-done
  550.0 7.9 collective-permute-done
  559.9 7.9 collective-permute-done
  569.8 7.9 collective-permute-done
  579.7 7.9 collective-permute-done
  589.6 7.9 collective-permute-done
  599.5 7.9 collective-permute-done
  609.4 7.9 collective-permute-done
  619.3 7.9 collective-permute-done
  629.2 7.9 collective-permute-done
  639.1 7.9 collective-permute-done
  649.0 7.9 collective-permute-done
  658.9 7.9 collective-permute-done
  672.4 133.6 %all-reduce.6.cloned.1.call-done = (f32[9,128,256]{1,2,0:T(8,128)}, f32[9,64,512]{2,1,0:T(8,128)}) async-done(((f32[9,128,256]{1,2,0:T(8,128)}, f32[9,64,512]{2,1,0:T(8,128)}), (f32[9,128,256]{1,2,0:T(8,128)}, f32[9,64,512]{2,1,0:T(8,128)})) %all-reduce.6.cloned.1.call-update) | async-done | bytes 2359312 | tf_op jit(solution)/shard_map/psum | solution.py:92
  (251 shorter events, 398.4 us)
Async XLA Ops:
  7.2 343.0 %all-gather.2.cloned.1.call-start = ((), (), s32[]{:S(2)}) async-start(), calls=%async_computation.2 | async-start | bytes 1310720 | tf_op jit(solution)/shard_map/all_gather | solution.py:88
  147.5 9.8 %collective-permute-start.1 = (f32[128,512]{1,0:T(8,128)S(1)}, f32[128,512]{1,0:T(8,128)S(1)}, u32[]{:S(2)}, u32[]{:S(2)}) collective-permute-start(f32[128,512]{1,0:T(8,128)S(1)} %multiply_add_fusion.8), channel_id=1, source_target_pairs={{0,4},{4,8},{8,12},{12,16},{16,20},{20,24},{24,28},{28,32},{32,36}... | collective-permute-start | bytes 786440 | tf_op jit(solution)/shard_map/while/body/eval_jaxpr/ppermute | solution.py:13
  157.4 9.8 %collective-permute-start.1 = (f32[128,512]{1,0:T(8,128)S(1)}, f32[128,512]{1,0:T(8,128)S(1)}, u32[]{:S(2)}, u32[]{:S(2)}) collective-permute-start(f32[128,512]{1,0:T(8,128)S(1)} %multiply_add_fusion.8), channel_id=1, source_target_pairs={{0,4},{4,8},{8,12},{12,16},{16,20},{20,24},{24,28},{28,32},{32,36}... | collective-permute-start | bytes 786440 | tf_op jit(solution)/shard_map/while/body/eval_jaxpr/ppermute | solution.py:13
  167.3 9.8 %collective-permute-start.1 = (f32[128,512]{1,0:T(8,128)S(1)}, f32[128,512]{1,0:T(8,128)S(1)}, u32[]{:S(2)}, u32[]{:S(2)}) collective-permute-start(f32[128,512]{1,0:T(8,128)S(1)} %multiply_add_fusion.8), channel_id=1, source_target_pairs={{0,4},{4,8},{8,12},{12,16},{16,20},{20,24},{24,28},{28,32},{32,36}... | collective-permute-start | bytes 786440 | tf_op jit(solution)/shard_map/while/body/eval_jaxpr/ppermute | solution.py:13
  177.2 9.8 %collective-permute-start.1 = (f32[128,512]{1,0:T(8,128)S(1)}, f32[128,512]{1,0:T(8,128)S(1)}, u32[]{:S(2)}, u32[]{:S(2)}) collective-permute-start(f32[128,512]{1,0:T(8,128)S(1)} %multiply_add_fusion.8), channel_id=1, source_target_pairs={{0,4},{4,8},{8,12},{12,16},{16,20},{20,24},{24,28},{28,32},{32,36}... | collective-permute-start | bytes 786440 | tf_op jit(solution)/shard_map/while/body/eval_jaxpr/ppermute | solution.py:13
  187.1 9.8 %collective-permute-start.1 = (f32[128,512]{1,0:T(8,128)S(1)}, f32[128,512]{1,0:T(8,128)S(1)}, u32[]{:S(2)}, u32[]{:S(2)}) collective-permute-start(f32[128,512]{1,0:T(8,128)S(1)} %multiply_add_fusion.8), channel_id=1, source_target_pairs={{0,4},{4,8},{8,12},{12,16},{16,20},{20,24},{24,28},{28,32},{32,36}... | collective-permute-start | bytes 786440 | tf_op jit(solution)/shard_map/while/body/eval_jaxpr/ppermute | solution.py:13
  197.0 9.8 %collective-permute-start.1 = (f32[128,512]{1,0:T(8,128)S(1)}, f32[128,512]{1,0:T(8,128)S(1)}, u32[]{:S(2)}, u32[]{:S(2)}) collective-permute-start(f32[128,512]{1,0:T(8,128)S(1)} %multiply_add_fusion.8), channel_id=1, source_target_pairs={{0,4},{4,8},{8,12},{12,16},{16,20},{20,24},{24,28},{28,32},{32,36}... | collective-permute-start | bytes 786440 | tf_op jit(solution)/shard_map/while/body/eval_jaxpr/ppermute | solution.py:13
  206.9 9.8 %collective-permute-start.1 = (f32[128,512]{1,0:T(8,128)S(1)}, f32[128,512]{1,0:T(8,128)S(1)}, u32[]{:S(2)}, u32[]{:S(2)}) collective-permute-start(f32[128,512]{1,0:T(8,128)S(1)} %multiply_add_fusion.8), channel_id=1, source_target_pairs={{0,4},{4,8},{8,12},{12,16},{16,20},{20,24},{24,28},{28,32},{32,36}... | collective-permute-start | bytes 786440 | tf_op jit(solution)/shard_map/while/body/eval_jaxpr/ppermute | solution.py:13
  216.8 9.8 %collective-permute-start.1 = (f32[128,512]{1,0:T(8,128)S(1)}, f32[128,512]{1,0:T(8,128)S(1)}, u32[]{:S(2)}, u32[]{:S(2)}) collective-permute-start(f32[128,512]{1,0:T(8,128)S(1)} %multiply_add_fusion.8), channel_id=1, source_target_pairs={{0,4},{4,8},{8,12},{12,16},{16,20},{20,24},{24,28},{28,32},{32,36}... | collective-permute-start | bytes 786440 | tf_op jit(solution)/shard_map/while/body/eval_jaxpr/ppermute | solution.py:13
  226.7 9.8 %collective-permute-start.1 = (f32[128,512]{1,0:T(8,128)S(1)}, f32[128,512]{1,0:T(8,128)S(1)}, u32[]{:S(2)}, u32[]{:S(2)}) collective-permute-start(f32[128,512]{1,0:T(8,128)S(1)} %multiply_add_fusion.8), channel_id=1, source_target_pairs={{0,4},{4,8},{8,12},{12,16},{16,20},{20,24},{24,28},{28,32},{32,36}... | collective-permute-start | bytes 786440 | tf_op jit(solution)/shard_map/while/body/eval_jaxpr/ppermute | solution.py:13
  236.6 9.8 %collective-permute-start.1 = (f32[128,512]{1,0:T(8,128)S(1)}, f32[128,512]{1,0:T(8,128)S(1)}, u32[]{:S(2)}, u32[]{:S(2)}) collective-permute-start(f32[128,512]{1,0:T(8,128)S(1)} %multiply_add_fusion.8), channel_id=1, source_target_pairs={{0,4},{4,8},{8,12},{12,16},{16,20},{20,24},{24,28},{28,32},{32,36}... | collective-permute-start | bytes 786440 | tf_op jit(solution)/shard_map/while/body/eval_jaxpr/ppermute | solution.py:13
  246.5 9.8 %collective-permute-start.1 = (f32[128,512]{1,0:T(8,128)S(1)}, f32[128,512]{1,0:T(8,128)S(1)}, u32[]{:S(2)}, u32[]{:S(2)}) collective-permute-start(f32[128,512]{1,0:T(8,128)S(1)} %multiply_add_fusion.8), channel_id=1, source_target_pairs={{0,4},{4,8},{8,12},{12,16},{16,20},{20,24},{24,28},{28,32},{32,36}... | collective-permute-start | bytes 786440 | tf_op jit(solution)/shard_map/while/body/eval_jaxpr/ppermute | solution.py:13
  256.4 9.8 %collective-permute-start.1 = (f32[128,512]{1,0:T(8,128)S(1)}, f32[128,512]{1,0:T(8,128)S(1)}, u32[]{:S(2)}, u32[]{:S(2)}) collective-permute-start(f32[128,512]{1,0:T(8,128)S(1)} %multiply_add_fusion.8), channel_id=1, source_target_pairs={{0,4},{4,8},{8,12},{12,16},{16,20},{20,24},{24,28},{28,32},{32,36}... | collective-permute-start | bytes 786440 | tf_op jit(solution)/shard_map/while/body/eval_jaxpr/ppermute | solution.py:13
  266.3 9.8 %collective-permute-start.1 = (f32[128,512]{1,0:T(8,128)S(1)}, f32[128,512]{1,0:T(8,128)S(1)}, u32[]{:S(2)}, u32[]{:S(2)}) collective-permute-start(f32[128,512]{1,0:T(8,128)S(1)} %multiply_add_fusion.8), channel_id=1, source_target_pairs={{0,4},{4,8},{8,12},{12,16},{16,20},{20,24},{24,28},{28,32},{32,36}... | collective-permute-start | bytes 786440 | tf_op jit(solution)/shard_map/while/body/eval_jaxpr/ppermute | solution.py:13
  276.2 9.8 %collective-permute-start.1 = (f32[128,512]{1,0:T(8,128)S(1)}, f32[128,512]{1,0:T(8,128)S(1)}, u32[]{:S(2)}, u32[]{:S(2)}) collective-permute-start(f32[128,512]{1,0:T(8,128)S(1)} %multiply_add_fusion.8), channel_id=1, source_target_pairs={{0,4},{4,8},{8,12},{12,16},{16,20},{20,24},{24,28},{28,32},{32,36}... | collective-permute-start | bytes 786440 | tf_op jit(solution)/shard_map/while/body/eval_jaxpr/ppermute | solution.py:13
  286.1 9.8 %collective-permute-start.1 = (f32[128,512]{1,0:T(8,128)S(1)}, f32[128,512]{1,0:T(8,128)S(1)}, u32[]{:S(2)}, u32[]{:S(2)}) collective-permute-start(f32[128,512]{1,0:T(8,128)S(1)} %multiply_add_fusion.8), channel_id=1, source_target_pairs={{0,4},{4,8},{8,12},{12,16},{16,20},{20,24},{24,28},{28,32},{32,36}... | collective-permute-start | bytes 786440 | tf_op jit(solution)/shard_map/while/body/eval_jaxpr/ppermute | solution.py:13
  296.7 88.0 %reduce-scatter.2.cloned.1.call-start = ((), (), s32[]{:S(2)}) async-start(), calls=%async_computation.1 | async-start | bytes 2621440 | tf_op jit(solution)/shard_map/reduce_scatter | solution.py:60
  300.2 505.8 %all-reduce.6.cloned.1.call-start = ((), (), s32[]{:S(2)}) async-start(), calls=%async_computation.3 | async-start | bytes 4718592 | tf_op jit(solution)/shard_map/psum | solution.py:92
  498.6 9.8 %collective-permute-start = (f32[128,512]{1,0:T(8,128)S(1)}, f32[128,512]{1,0:T(8,128)S(1)}, u32[]{:S(2)}, u32[]{:S(2)}) collective-permute-start(f32[128,512]{1,0:T(8,128)S(1)} %multiply_add_fusion.7), channel_id=1, source_target_pairs={{4,0},{8,4},{12,8},{16,12},{20,16},{24,20},{28,24},{32,28},{36,32}... | collective-permute-start | bytes 786440 | tf_op jit(solution)/shard_map/while/body/eval_jaxpr/ppermute | solution.py:13
  508.5 9.8 %collective-permute-start = (f32[128,512]{1,0:T(8,128)S(1)}, f32[128,512]{1,0:T(8,128)S(1)}, u32[]{:S(2)}, u32[]{:S(2)}) collective-permute-start(f32[128,512]{1,0:T(8,128)S(1)} %multiply_add_fusion.7), channel_id=1, source_target_pairs={{4,0},{8,4},{12,8},{16,12},{20,16},{24,20},{28,24},{32,28},{36,32}... | collective-permute-start | bytes 786440 | tf_op jit(solution)/shard_map/while/body/eval_jaxpr/ppermute | solution.py:13
  518.4 9.8 %collective-permute-start = (f32[128,512]{1,0:T(8,128)S(1)}, f32[128,512]{1,0:T(8,128)S(1)}, u32[]{:S(2)}, u32[]{:S(2)}) collective-permute-start(f32[128,512]{1,0:T(8,128)S(1)} %multiply_add_fusion.7), channel_id=1, source_target_pairs={{4,0},{8,4},{12,8},{16,12},{20,16},{24,20},{28,24},{32,28},{36,32}... | collective-permute-start | bytes 786440 | tf_op jit(solution)/shard_map/while/body/eval_jaxpr/ppermute | solution.py:13
  528.3 9.8 %collective-permute-start = (f32[128,512]{1,0:T(8,128)S(1)}, f32[128,512]{1,0:T(8,128)S(1)}, u32[]{:S(2)}, u32[]{:S(2)}) collective-permute-start(f32[128,512]{1,0:T(8,128)S(1)} %multiply_add_fusion.7), channel_id=1, source_target_pairs={{4,0},{8,4},{12,8},{16,12},{20,16},{24,20},{28,24},{32,28},{36,32}... | collective-permute-start | bytes 786440 | tf_op jit(solution)/shard_map/while/body/eval_jaxpr/ppermute | solution.py:13
  538.2 9.8 %collective-permute-start = (f32[128,512]{1,0:T(8,128)S(1)}, f32[128,512]{1,0:T(8,128)S(1)}, u32[]{:S(2)}, u32[]{:S(2)}) collective-permute-start(f32[128,512]{1,0:T(8,128)S(1)} %multiply_add_fusion.7), channel_id=1, source_target_pairs={{4,0},{8,4},{12,8},{16,12},{20,16},{24,20},{28,24},{32,28},{36,32}... | collective-permute-start | bytes 786440 | tf_op jit(solution)/shard_map/while/body/eval_jaxpr/ppermute | solution.py:13
  548.1 9.8 %collective-permute-start = (f32[128,512]{1,0:T(8,128)S(1)}, f32[128,512]{1,0:T(8,128)S(1)}, u32[]{:S(2)}, u32[]{:S(2)}) collective-permute-start(f32[128,512]{1,0:T(8,128)S(1)} %multiply_add_fusion.7), channel_id=1, source_target_pairs={{4,0},{8,4},{12,8},{16,12},{20,16},{24,20},{28,24},{32,28},{36,32}... | collective-permute-start | bytes 786440 | tf_op jit(solution)/shard_map/while/body/eval_jaxpr/ppermute | solution.py:13
  558.0 9.8 %collective-permute-start = (f32[128,512]{1,0:T(8,128)S(1)}, f32[128,512]{1,0:T(8,128)S(1)}, u32[]{:S(2)}, u32[]{:S(2)}) collective-permute-start(f32[128,512]{1,0:T(8,128)S(1)} %multiply_add_fusion.7), channel_id=1, source_target_pairs={{4,0},{8,4},{12,8},{16,12},{20,16},{24,20},{28,24},{32,28},{36,32}... | collective-permute-start | bytes 786440 | tf_op jit(solution)/shard_map/while/body/eval_jaxpr/ppermute | solution.py:13
  567.9 9.8 %collective-permute-start = (f32[128,512]{1,0:T(8,128)S(1)}, f32[128,512]{1,0:T(8,128)S(1)}, u32[]{:S(2)}, u32[]{:S(2)}) collective-permute-start(f32[128,512]{1,0:T(8,128)S(1)} %multiply_add_fusion.7), channel_id=1, source_target_pairs={{4,0},{8,4},{12,8},{16,12},{20,16},{24,20},{28,24},{32,28},{36,32}... | collective-permute-start | bytes 786440 | tf_op jit(solution)/shard_map/while/body/eval_jaxpr/ppermute | solution.py:13
  577.8 9.8 %collective-permute-start = (f32[128,512]{1,0:T(8,128)S(1)}, f32[128,512]{1,0:T(8,128)S(1)}, u32[]{:S(2)}, u32[]{:S(2)}) collective-permute-start(f32[128,512]{1,0:T(8,128)S(1)} %multiply_add_fusion.7), channel_id=1, source_target_pairs={{4,0},{8,4},{12,8},{16,12},{20,16},{24,20},{28,24},{32,28},{36,32}... | collective-permute-start | bytes 786440 | tf_op jit(solution)/shard_map/while/body/eval_jaxpr/ppermute | solution.py:13
  587.7 9.8 %collective-permute-start = (f32[128,512]{1,0:T(8,128)S(1)}, f32[128,512]{1,0:T(8,128)S(1)}, u32[]{:S(2)}, u32[]{:S(2)}) collective-permute-start(f32[128,512]{1,0:T(8,128)S(1)} %multiply_add_fusion.7), channel_id=1, source_target_pairs={{4,0},{8,4},{12,8},{16,12},{20,16},{24,20},{28,24},{32,28},{36,32}... | collective-permute-start | bytes 786440 | tf_op jit(solution)/shard_map/while/body/eval_jaxpr/ppermute | solution.py:13
  597.6 9.8 %collective-permute-start = (f32[128,512]{1,0:T(8,128)S(1)}, f32[128,512]{1,0:T(8,128)S(1)}, u32[]{:S(2)}, u32[]{:S(2)}) collective-permute-start(f32[128,512]{1,0:T(8,128)S(1)} %multiply_add_fusion.7), channel_id=1, source_target_pairs={{4,0},{8,4},{12,8},{16,12},{20,16},{24,20},{28,24},{32,28},{36,32}... | collective-permute-start | bytes 786440 | tf_op jit(solution)/shard_map/while/body/eval_jaxpr/ppermute | solution.py:13
  607.5 9.8 %collective-permute-start = (f32[128,512]{1,0:T(8,128)S(1)}, f32[128,512]{1,0:T(8,128)S(1)}, u32[]{:S(2)}, u32[]{:S(2)}) collective-permute-start(f32[128,512]{1,0:T(8,128)S(1)} %multiply_add_fusion.7), channel_id=1, source_target_pairs={{4,0},{8,4},{12,8},{16,12},{20,16},{24,20},{28,24},{32,28},{36,32}... | collective-permute-start | bytes 786440 | tf_op jit(solution)/shard_map/while/body/eval_jaxpr/ppermute | solution.py:13
  627.3 9.8 %collective-permute-start = (f32[128,512]{1,0:T(8,128)S(1)}, f32[128,512]{1,0:T(8,128)S(1)}, u32[]{:S(2)}, u32[]{:S(2)}) collective-permute-start(f32[128,512]{1,0:T(8,128)S(1)} %multiply_add_fusion.7), channel_id=1, source_target_pairs={{4,0},{8,4},{12,8},{16,12},{20,16},{24,20},{28,24},{32,28},{36,32}... | collective-permute-start | bytes 786440 | tf_op jit(solution)/shard_map/while/body/eval_jaxpr/ppermute | solution.py:13
  647.1 9.8 %collective-permute-start = (f32[128,512]{1,0:T(8,128)S(1)}, f32[128,512]{1,0:T(8,128)S(1)}, u32[]{:S(2)}, u32[]{:S(2)}) collective-permute-start(f32[128,512]{1,0:T(8,128)S(1)} %multiply_add_fusion.7), channel_id=1, source_target_pairs={{4,0},{8,4},{12,8},{16,12},{20,16},{24,20},{28,24},{32,28},{36,32}... | collective-permute-start | bytes 786440 | tf_op jit(solution)/shard_map/while/body/eval_jaxpr/ppermute | solution.py:13
  (41 other events, 858.8 us)
Sparse Core Ops, SparseCore 0:
  296.9 53.3 all-gather.1
  352.6 32.0 reduce-scatter.1
  671.7 134.1 all-reduce.5
where the time goes:
time: 820 us; the launch traced here: 818 us
  waiting for transfers between devices  525 us (64%)
  starting transfers between devices  230 us (28%)
  other arithmetic  24.4 us (3%)
  between operations  14.1 us (2%)
  matrix products  12.6 us (2%)
  local copies, waits for them, and re-layouts  9.91 us (1%)
    ppermute x62, waiting for transfers between devices, passed_along(): lax.ppermute(value, axis, [(source, source + steps) for source in range(f...  318 us
    ppermute x62, starting transfers between devices, passed_along(): lax.ppermute(value, axis, [(source, source + steps) for source in range(f...  230 us
    psum x1, waiting for transfers between devices, body(): grad_b, grad_c = lax.psum((grad_b_part, grad_c_part), 'tm')  134 us
    all_gather x1, waiting for transfers between devices, body(): lax.all_gather(states_bf, 'chan', axis=1, tiled=True)  49.7 us
    reduce_scatter x1, waiting for transfers between devices, body(): lax.psum_scatter(jnp.einsum('kup,fkus->pfs', kernel_c, cot_stack, preferr...  23.6 us
  transfers between devices with their start and end apart: 65, of which 65 were waited for; matrix products, arithmetic and copies ran while one was open for 2% of the time, Pallas kernels for 0%

commit v1 on v0

--- a/solution.py
+++ b/solution.py
@@ -5,6 +5,24 @@
 
 W = 64
 offsets = ((-1, -1), (-1, 0), (-1, 1), (0, -1), (0, 0), (0, 1), (1, -1), (1, 0), (1, 1))
+
+
+def gather_around(value, axis, dim):
+    ways, here, step = (lax.axis_size(axis), lax.axis_index(axis), value.shape[dim])
+    shape = [n * ways if d == dim else n for d, n in enumerate(value.shape)]
+    full = lax.dynamic_update_slice_in_dim(
+        jnp.zeros(shape, value.dtype), value, here * step, axis=dim
+    )
+    going_up = going_down = value
+    for far in range(1, ways // 2 + 1):
+        going_up = lax.ppermute(going_up, axis, [(d, (d + 1) % ways) for d in range(ways)])
+        full = lax.dynamic_update_slice_in_dim(full, going_up, (here - far) % ways * step, axis=dim)
+        if 2 * far < ways:
+            going_down = lax.ppermute(going_down, axis, [(d, (d - 1) % ways) for d in range(ways)])
+            full = lax.dynamic_update_slice_in_dim(
+                full, going_down, (here + far) % ways * step, axis=dim
+            )
+    return full
 
 
 def passed_along(value, axis, steps):
@@ -85,7 +103,7 @@
     grad_b_part = jnp.einsum(
         "fps,fkcs->kpc", adjoint_bf, input_stack, preferred_element_type=jnp.float32
     )
-    shifted = stencil_stack(lax.all_gather(states_bf, "chan", axis=1, tiled=True), W, 1)
+    shifted = stencil_stack(gather_around(states_bf, "chan", 1), W, 1)
     grad_c_part = jnp.einsum(
         "fus,fkps->kup", cotangent, shifted, preferred_element_type=jnp.float32
     )

time: 820 us -> 791 us (0.965)
  waiting for transfers between devices: 525 us -> 494 us
    all_gather x1 -> x0, waiting for transfers between devices: 49.7 us -> none  [body(): lax.all_gather(states_bf, 'chan', axis=1, tiled=True)]
    ppermute x62, waiting for transfers between devices: 318 us -> 351 us  [passed_along(): lax.ppermute(value, axis, [(source, source + steps) for source in range(f...]
    reduce_scatter x1, waiting for transfers between devices: 23.6 us -> 0.01 us  [body(): lax.psum_scatter(jnp.einsum('kup,fkus->pfs', kernel_c, cot_stack, preferr...]
    ppermute x0 -> x3, waiting for transfers between devices: none -> 10.4 us  [the longest x2 10.4 us: gather_around(): lax.ppermute(going_up, axis, [(d, (d + 1) % ways) for d in range(ways)])]
  transfers between devices with their start and end apart: 65 -> 67, of which waited for: 65 -> 65; matrix products, arithmetic and copies ran while one was open for 2% -> 2% of each run, Pallas kernels for 0% -> 0%
where the time goes in v1:
time: 791 us; the launch traced here: 789 us
  waiting for transfers between devices  494 us (62%)
  starting transfers between devices  233 us (29%)
  other arithmetic  23.3 us (3%)
  between operations  14.4 us (2%)
  matrix products  12.6 us (2%)
  local copies, waits for them, and re-layouts  10.1 us (1%)
    ppermute x62, waiting for transfers between devices, passed_along(): lax.ppermute(value, axis, [(source, source + steps) for source in range(f...  351 us
    ppermute x62, starting transfers between devices, passed_along(): lax.ppermute(value, axis, [(source, source + steps) for source in range(f...  229 us
    psum x1, waiting for transfers between devices, body(): grad_b, grad_c = lax.psum((grad_b_part, grad_c_part), 'tm')  132 us
  transfers between devices with their start and end apart: 67, of which 65 were waited for; matrix products, arithmetic and copies ran while one was open for 2% of the time, Pallas kernels for 0%

profile of v1, /device:TPU:1, one launch (start us, length us, event | category | flops | bytes accessed | tf_op | source)
XLA Modules:
  0.0 789.4 jit_solution(17027303213106961504)
XLA Ops:
  25.6 275.2 %while.51 = (s32[]{:T(128)}, f32[128,512]{1,0:T(8,128)S(1)}, f32[128]{0:T(128)S(1)}, f32[128,512]{1,0:T(8,128)S(1)}, s32[]{:T(128)}) while((s32[]{:T(128)}, f32[128,512]{1,0:T(8,128)S(1)}, f32[128]{0:T(128)S(1)}, f32[128,512]{1,0:T(8,128)S(1)}, s32[]{:T(128)}) %tuple.102), condition=%wide.region_12.13_spmd, body=%wide.region_11.12_spmd.sunk | while | flops 131074 | bytes 1835621 | solution.py:72
  202.0 6.5 collective-permute-start.1
  327.3 312.3 %while.50 = (s32[]{:T(128)}, f32[128,512]{1,0:T(8,128)S(1)}, f32[128]{0:T(128)S(1)}, f32[128,512]{1,0:T(8,128)S(1)}, s32[]{:T(128)}) while((s32[]{:T(128)}, f32[128,512]{1,0:T(8,128)S(1)}, f32[128]{0:T(128)S(1)}, f32[128,512]{1,0:T(8,128)S(1)}, s32[]{:T(128)}) %tuple.112), condition=%wide.region_6.7_spmd, body=%wide.region_5.6_spmd.sunk | while | flops 131074 | bytes 1835621 | solution.py:97
  329.3 10.6 %collective-permute-done = f32[128,512]{1,0:T(8,128)S(1)} collective-permute-done((f32[128,512]{1,0:T(8,128)S(1)}, f32[128,512]{1,0:T(8,128)S(1)}, u32[]{:S(2)}, u32[]{:S(2)}) %collective-permute-start) | collective-permute-done | bytes 262176 | tf_op jit(solution)/shard_map/while/body/eval_jaxpr/ppermute | solution.py:31
  349.7 10.6 %collective-permute-done = f32[128,512]{1,0:T(8,128)S(1)} collective-permute-done((f32[128,512]{1,0:T(8,128)S(1)}, f32[128,512]{1,0:T(8,128)S(1)}, u32[]{:S(2)}, u32[]{:S(2)}) %collective-permute-start) | collective-permute-done | bytes 262176 | tf_op jit(solution)/shard_map/while/body/eval_jaxpr/ppermute | solution.py:31
  370.1 10.6 %collective-permute-done = f32[128,512]{1,0:T(8,128)S(1)} collective-permute-done((f32[128,512]{1,0:T(8,128)S(1)}, f32[128,512]{1,0:T(8,128)S(1)}, u32[]{:S(2)}, u32[]{:S(2)}) %collective-permute-start) | collective-permute-done | bytes 262176 | tf_op jit(solution)/shard_map/while/body/eval_jaxpr/ppermute | solution.py:31
  390.5 11.5 %collective-permute-done = f32[128,512]{1,0:T(8,128)S(1)} collective-permute-done((f32[128,512]{1,0:T(8,128)S(1)}, f32[128,512]{1,0:T(8,128)S(1)}, u32[]{:S(2)}, u32[]{:S(2)}) %collective-permute-start) | collective-permute-done | bytes 262176 | tf_op jit(solution)/shard_map/while/body/eval_jaxpr/ppermute | solution.py:31
  404.0 7.9 collective-permute-done
  413.9 7.9 collective-permute-done
  423.8 7.9 collective-permute-done
  433.7 7.9 collective-permute-done
  443.6 7.9 collective-permute-done
  453.5 7.9 collective-permute-done
  463.4 7.9 collective-permute-done
  473.3 7.9 collective-permute-done
  483.2 7.9 collective-permute-done
  493.1 7.9 collective-permute-done
  503.0 7.9 collective-permute-done
  512.9 7.9 collective-permute-done
  522.8 7.9 collective-permute-done
  532.7 7.9 collective-permute-done
  542.6 7.9 collective-permute-done
  552.5 7.9 collective-permute-done
  562.4 7.9 collective-permute-done
  572.3 7.9 collective-permute-done
  582.2 7.9 collective-permute-done
  592.1 7.9 collective-permute-done
  602.0 7.9 collective-permute-done
  611.8 7.9 collective-permute-done
  621.7 7.9 collective-permute-done
  631.6 7.9 collective-permute-done
  645.2 132.3 %all-reduce.6.cloned.1.call-done = (f32[9,128,256]{1,2,0:T(8,128)}, f32[9,64,512]{2,1,0:T(8,128)}) async-done(((f32[9,128,256]{1,2,0:T(8,128)}, f32[9,64,512]{2,1,0:T(8,128)}), (f32[9,128,256]{1,2,0:T(8,128)}, f32[9,64,512]{2,1,0:T(8,128)})) %all-reduce.6.cloned.1.call-update) | async-done | bytes 2359312 | tf_op jit(solution)/shard_map/psum | solution.py:110
  (256 shorter events, 405.9 us)
Async XLA Ops:
  7.2 317.4 %reduce-scatter.2.cloned.1.call-start = ((), (), s32[]{:S(2)}) async-start(), calls=%async_computation.1 | async-start | bytes 2621440 | tf_op jit(solution)/shard_map/reduce_scatter | solution.py:78
  18.8 758.7 %all-reduce.6.cloned.1.call-start = ((), (), s32[]{:S(2)}) async-start(), calls=%async_computation.2 | async-start | bytes 4718592 | tf_op jit(solution)/shard_map/psum | solution.py:110
  152.5 9.8 %collective-permute-start.1 = (f32[128,512]{1,0:T(8,128)S(1)}, f32[128,512]{1,0:T(8,128)S(1)}, u32[]{:S(2)}, u32[]{:S(2)}) collective-permute-start(f32[128,512]{1,0:T(8,128)S(1)} %multiply_add_fusion.8), channel_id=1, source_target_pairs={{0,4},{4,8},{8,12},{12,16},{16,20},{20,24},{24,28},{28,32},{32,36}... | collective-permute-start | bytes 786440 | tf_op jit(solution)/shard_map/while/body/eval_jaxpr/ppermute | solution.py:31
  162.4 9.8 %collective-permute-start.1 = (f32[128,512]{1,0:T(8,128)S(1)}, f32[128,512]{1,0:T(8,128)S(1)}, u32[]{:S(2)}, u32[]{:S(2)}) collective-permute-start(f32[128,512]{1,0:T(8,128)S(1)} %multiply_add_fusion.8), channel_id=1, source_target_pairs={{0,4},{4,8},{8,12},{12,16},{16,20},{20,24},{24,28},{28,32},{32,36}... | collective-permute-start | bytes 786440 | tf_op jit(solution)/shard_map/while/body/eval_jaxpr/ppermute | solution.py:31
  172.3 9.8 %collective-permute-start.1 = (f32[128,512]{1,0:T(8,128)S(1)}, f32[128,512]{1,0:T(8,128)S(1)}, u32[]{:S(2)}, u32[]{:S(2)}) collective-permute-start(f32[128,512]{1,0:T(8,128)S(1)} %multiply_add_fusion.8), channel_id=1, source_target_pairs={{0,4},{4,8},{8,12},{12,16},{16,20},{20,24},{24,28},{28,32},{32,36}... | collective-permute-start | bytes 786440 | tf_op jit(solution)/shard_map/while/body/eval_jaxpr/ppermute | solution.py:31
  182.2 9.8 %collective-permute-start.1 = (f32[128,512]{1,0:T(8,128)S(1)}, f32[128,512]{1,0:T(8,128)S(1)}, u32[]{:S(2)}, u32[]{:S(2)}) collective-permute-start(f32[128,512]{1,0:T(8,128)S(1)} %multiply_add_fusion.8), channel_id=1, source_target_pairs={{0,4},{4,8},{8,12},{12,16},{16,20},{20,24},{24,28},{28,32},{32,36}... | collective-permute-start | bytes 786440 | tf_op jit(solution)/shard_map/while/body/eval_jaxpr/ppermute | solution.py:31
  192.1 9.8 %collective-permute-start.1 = (f32[128,512]{1,0:T(8,128)S(1)}, f32[128,512]{1,0:T(8,128)S(1)}, u32[]{:S(2)}, u32[]{:S(2)}) collective-permute-start(f32[128,512]{1,0:T(8,128)S(1)} %multiply_add_fusion.8), channel_id=1, source_target_pairs={{0,4},{4,8},{8,12},{12,16},{16,20},{20,24},{24,28},{28,32},{32,36}... | collective-permute-start | bytes 786440 | tf_op jit(solution)/shard_map/while/body/eval_jaxpr/ppermute | solution.py:31
  202.0 9.8 %collective-permute-start.1 = (f32[128,512]{1,0:T(8,128)S(1)}, f32[128,512]{1,0:T(8,128)S(1)}, u32[]{:S(2)}, u32[]{:S(2)}) collective-permute-start(f32[128,512]{1,0:T(8,128)S(1)} %multiply_add_fusion.8), channel_id=1, source_target_pairs={{0,4},{4,8},{8,12},{12,16},{16,20},{20,24},{24,28},{28,32},{32,36}... | collective-permute-start | bytes 786440 | tf_op jit(solution)/shard_map/while/body/eval_jaxpr/ppermute | solution.py:31
  211.9 9.8 %collective-permute-start.1 = (f32[128,512]{1,0:T(8,128)S(1)}, f32[128,512]{1,0:T(8,128)S(1)}, u32[]{:S(2)}, u32[]{:S(2)}) collective-permute-start(f32[128,512]{1,0:T(8,128)S(1)} %multiply_add_fusion.8), channel_id=1, source_target_pairs={{0,4},{4,8},{8,12},{12,16},{16,20},{20,24},{24,28},{28,32},{32,36}... | collective-permute-start | bytes 786440 | tf_op jit(solution)/shard_map/while/body/eval_jaxpr/ppermute | solution.py:31
  221.8 9.8 %collective-permute-start.1 = (f32[128,512]{1,0:T(8,128)S(1)}, f32[128,512]{1,0:T(8,128)S(1)}, u32[]{:S(2)}, u32[]{:S(2)}) collective-permute-start(f32[128,512]{1,0:T(8,128)S(1)} %multiply_add_fusion.8), channel_id=1, source_target_pairs={{0,4},{4,8},{8,12},{12,16},{16,20},{20,24},{24,28},{28,32},{32,36}... | collective-permute-start | bytes 786440 | tf_op jit(solution)/shard_map/while/body/eval_jaxpr/ppermute | solution.py:31
  231.7 9.8 %collective-permute-start.1 = (f32[128,512]{1,0:T(8,128)S(1)}, f32[128,512]{1,0:T(8,128)S(1)}, u32[]{:S(2)}, u32[]{:S(2)}) collective-permute-start(f32[128,512]{1,0:T(8,128)S(1)} %multiply_add_fusion.8), channel_id=1, source_target_pairs={{0,4},{4,8},{8,12},{12,16},{16,20},{20,24},{24,28},{28,32},{32,36}... | collective-permute-start | bytes 786440 | tf_op jit(solution)/shard_map/while/body/eval_jaxpr/ppermute | solution.py:31
  241.6 9.8 %collective-permute-start.1 = (f32[128,512]{1,0:T(8,128)S(1)}, f32[128,512]{1,0:T(8,128)S(1)}, u32[]{:S(2)}, u32[]{:S(2)}) collective-permute-start(f32[128,512]{1,0:T(8,128)S(1)} %multiply_add_fusion.8), channel_id=1, source_target_pairs={{0,4},{4,8},{8,12},{12,16},{16,20},{20,24},{24,28},{28,32},{32,36}... | collective-permute-start | bytes 786440 | tf_op jit(solution)/shard_map/while/body/eval_jaxpr/ppermute | solution.py:31
  251.5 9.8 %collective-permute-start.1 = (f32[128,512]{1,0:T(8,128)S(1)}, f32[128,512]{1,0:T(8,128)S(1)}, u32[]{:S(2)}, u32[]{:S(2)}) collective-permute-start(f32[128,512]{1,0:T(8,128)S(1)} %multiply_add_fusion.8), channel_id=1, source_target_pairs={{0,4},{4,8},{8,12},{12,16},{16,20},{20,24},{24,28},{28,32},{32,36}... | collective-permute-start | bytes 786440 | tf_op jit(solution)/shard_map/while/body/eval_jaxpr/ppermute | solution.py:31
  261.4 9.8 %collective-permute-start.1 = (f32[128,512]{1,0:T(8,128)S(1)}, f32[128,512]{1,0:T(8,128)S(1)}, u32[]{:S(2)}, u32[]{:S(2)}) collective-permute-start(f32[128,512]{1,0:T(8,128)S(1)} %multiply_add_fusion.8), channel_id=1, source_target_pairs={{0,4},{4,8},{8,12},{12,16},{16,20},{20,24},{24,28},{28,32},{32,36}... | collective-permute-start | bytes 786440 | tf_op jit(solution)/shard_map/while/body/eval_jaxpr/ppermute | solution.py:31
  271.3 9.8 %collective-permute-start.1 = (f32[128,512]{1,0:T(8,128)S(1)}, f32[128,512]{1,0:T(8,128)S(1)}, u32[]{:S(2)}, u32[]{:S(2)}) collective-permute-start(f32[128,512]{1,0:T(8,128)S(1)} %multiply_add_fusion.8), channel_id=1, source_target_pairs={{0,4},{4,8},{8,12},{12,16},{16,20},{20,24},{24,28},{28,32},{32,36}... | collective-permute-start | bytes 786440 | tf_op jit(solution)/shard_map/while/body/eval_jaxpr/ppermute | solution.py:31
  281.2 9.8 %collective-permute-start.1 = (f32[128,512]{1,0:T(8,128)S(1)}, f32[128,512]{1,0:T(8,128)S(1)}, u32[]{:S(2)}, u32[]{:S(2)}) collective-permute-start(f32[128,512]{1,0:T(8,128)S(1)} %multiply_add_fusion.8), channel_id=1, source_target_pairs={{0,4},{4,8},{8,12},{12,16},{16,20},{20,24},{24,28},{28,32},{32,36}... | collective-permute-start | bytes 786440 | tf_op jit(solution)/shard_map/while/body/eval_jaxpr/ppermute | solution.py:31
  291.0 9.8 %collective-permute-start.1 = (f32[128,512]{1,0:T(8,128)S(1)}, f32[128,512]{1,0:T(8,128)S(1)}, u32[]{:S(2)}, u32[]{:S(2)}) collective-permute-start(f32[128,512]{1,0:T(8,128)S(1)} %multiply_add_fusion.8), channel_id=1, source_target_pairs={{0,4},{4,8},{8,12},{12,16},{16,20},{20,24},{24,28},{28,32},{32,36}... | collective-permute-start | bytes 786440 | tf_op jit(solution)/shard_map/while/body/eval_jaxpr/ppermute | solution.py:31
  327.4 12.5 %collective-permute-start = (f32[128,512]{1,0:T(8,128)S(1)}, f32[128,512]{1,0:T(8,128)S(1)}, u32[]{:S(2)}, u32[]{:S(2)}) collective-permute-start(f32[128,512]{1,0:T(8,128)S(1)} %multiply_add_fusion.7), channel_id=1, source_target_pairs={{4,0},{8,4},{12,8},{16,12},{20,16},{24,20},{28,24},{32,28},{36,32}... | collective-permute-start | bytes 786440 | tf_op jit(solution)/shard_map/while/body/eval_jaxpr/ppermute | solution.py:31
  347.8 12.5 %collective-permute-start = (f32[128,512]{1,0:T(8,128)S(1)}, f32[128,512]{1,0:T(8,128)S(1)}, u32[]{:S(2)}, u32[]{:S(2)}) collective-permute-start(f32[128,512]{1,0:T(8,128)S(1)} %multiply_add_fusion.7), channel_id=1, source_target_pairs={{4,0},{8,4},{12,8},{16,12},{20,16},{24,20},{28,24},{32,28},{36,32}... | collective-permute-start | bytes 786440 | tf_op jit(solution)/shard_map/while/body/eval_jaxpr/ppermute | solution.py:31
  368.2 12.5 %collective-permute-start = (f32[128,512]{1,0:T(8,128)S(1)}, f32[128,512]{1,0:T(8,128)S(1)}, u32[]{:S(2)}, u32[]{:S(2)}) collective-permute-start(f32[128,512]{1,0:T(8,128)S(1)} %multiply_add_fusion.7), channel_id=1, source_target_pairs={{4,0},{8,4},{12,8},{16,12},{20,16},{24,20},{28,24},{32,28},{36,32}... | collective-permute-start | bytes 786440 | tf_op jit(solution)/shard_map/while/body/eval_jaxpr/ppermute | solution.py:31
  388.6 13.4 %collective-permute-start = (f32[128,512]{1,0:T(8,128)S(1)}, f32[128,512]{1,0:T(8,128)S(1)}, u32[]{:S(2)}, u32[]{:S(2)}) collective-permute-start(f32[128,512]{1,0:T(8,128)S(1)} %multiply_add_fusion.7), channel_id=1, source_target_pairs={{4,0},{8,4},{12,8},{16,12},{20,16},{24,20},{28,24},{32,28},{36,32}... | collective-permute-start | bytes 786440 | tf_op jit(solution)/shard_map/while/body/eval_jaxpr/ppermute | solution.py:31
  402.1 9.8 %collective-permute-start = (f32[128,512]{1,0:T(8,128)S(1)}, f32[128,512]{1,0:T(8,128)S(1)}, u32[]{:S(2)}, u32[]{:S(2)}) collective-permute-start(f32[128,512]{1,0:T(8,128)S(1)} %multiply_add_fusion.7), channel_id=1, source_target_pairs={{4,0},{8,4},{12,8},{16,12},{20,16},{24,20},{28,24},{32,28},{36,32}... | collective-permute-start | bytes 786440 | tf_op jit(solution)/shard_map/while/body/eval_jaxpr/ppermute | solution.py:31
  412.0 9.8 %collective-permute-start = (f32[128,512]{1,0:T(8,128)S(1)}, f32[128,512]{1,0:T(8,128)S(1)}, u32[]{:S(2)}, u32[]{:S(2)}) collective-permute-start(f32[128,512]{1,0:T(8,128)S(1)} %multiply_add_fusion.7), channel_id=1, source_target_pairs={{4,0},{8,4},{12,8},{16,12},{20,16},{24,20},{28,24},{32,28},{36,32}... | collective-permute-start | bytes 786440 | tf_op jit(solution)/shard_map/while/body/eval_jaxpr/ppermute | solution.py:31
  421.9 9.8 %collective-permute-start = (f32[128,512]{1,0:T(8,128)S(1)}, f32[128,512]{1,0:T(8,128)S(1)}, u32[]{:S(2)}, u32[]{:S(2)}) collective-permute-start(f32[128,512]{1,0:T(8,128)S(1)} %multiply_add_fusion.7), channel_id=1, source_target_pairs={{4,0},{8,4},{12,8},{16,12},{20,16},{24,20},{28,24},{32,28},{36,32}... | collective-permute-start | bytes 786440 | tf_op jit(solution)/shard_map/while/body/eval_jaxpr/ppermute | solution.py:31
  431.8 9.8 %collective-permute-start = (f32[128,512]{1,0:T(8,128)S(1)}, f32[128,512]{1,0:T(8,128)S(1)}, u32[]{:S(2)}, u32[]{:S(2)}) collective-permute-start(f32[128,512]{1,0:T(8,128)S(1)} %multiply_add_fusion.7), channel_id=1, source_target_pairs={{4,0},{8,4},{12,8},{16,12},{20,16},{24,20},{28,24},{32,28},{36,32}... | collective-permute-start | bytes 786440 | tf_op jit(solution)/shard_map/while/body/eval_jaxpr/ppermute | solution.py:31
  441.7 9.8 %collective-permute-start = (f32[128,512]{1,0:T(8,128)S(1)}, f32[128,512]{1,0:T(8,128)S(1)}, u32[]{:S(2)}, u32[]{:S(2)}) collective-permute-start(f32[128,512]{1,0:T(8,128)S(1)} %multiply_add_fusion.7), channel_id=1, source_target_pairs={{4,0},{8,4},{12,8},{16,12},{20,16},{24,20},{28,24},{32,28},{36,32}... | collective-permute-start | bytes 786440 | tf_op jit(solution)/shard_map/while/body/eval_jaxpr/ppermute | solution.py:31
  451.6 9.8 %collective-permute-start = (f32[128,512]{1,0:T(8,128)S(1)}, f32[128,512]{1,0:T(8,128)S(1)}, u32[]{:S(2)}, u32[]{:S(2)}) collective-permute-start(f32[128,512]{1,0:T(8,128)S(1)} %multiply_add_fusion.7), channel_id=1, source_target_pairs={{4,0},{8,4},{12,8},{16,12},{20,16},{24,20},{28,24},{32,28},{36,32}... | collective-permute-start | bytes 786440 | tf_op jit(solution)/shard_map/while/body/eval_jaxpr/ppermute | solution.py:31
  471.4 9.8 %collective-permute-start = (f32[128,512]{1,0:T(8,128)S(1)}, f32[128,512]{1,0:T(8,128)S(1)}, u32[]{:S(2)}, u32[]{:S(2)}) collective-permute-start(f32[128,512]{1,0:T(8,128)S(1)} %multiply_add_fusion.7), channel_id=1, source_target_pairs={{4,0},{8,4},{12,8},{16,12},{20,16},{24,20},{28,24},{32,28},{36,32}... | collective-permute-start | bytes 786440 | tf_op jit(solution)/shard_map/while/body/eval_jaxpr/ppermute | solution.py:31
  491.2 9.8 %collective-permute-start = (f32[128,512]{1,0:T(8,128)S(1)}, f32[128,512]{1,0:T(8,128)S(1)}, u32[]{:S(2)}, u32[]{:S(2)}) collective-permute-start(f32[128,512]{1,0:T(8,128)S(1)} %multiply_add_fusion.7), channel_id=1, source_target_pairs={{4,0},{8,4},{12,8},{16,12},{20,16},{24,20},{28,24},{32,28},{36,32}... | collective-permute-start | bytes 786440 | tf_op jit(solution)/shard_map/while/body/eval_jaxpr/ppermute | solution.py:31
  511.0 9.8 %collective-permute-start = (f32[128,512]{1,0:T(8,128)S(1)}, f32[128,512]{1,0:T(8,128)S(1)}, u32[]{:S(2)}, u32[]{:S(2)}) collective-permute-start(f32[128,512]{1,0:T(8,128)S(1)} %multiply_add_fusion.7), channel_id=1, source_target_pairs={{4,0},{8,4},{12,8},{16,12},{20,16},{24,20},{28,24},{32,28},{36,32}... | collective-permute-start | bytes 786440 | tf_op jit(solution)/shard_map/while/body/eval_jaxpr/ppermute | solution.py:31
  530.8 9.8 %collective-permute-start = (f32[128,512]{1,0:T(8,128)S(1)}, f32[128,512]{1,0:T(8,128)S(1)}, u32[]{:S(2)}, u32[]{:S(2)}) collective-permute-start(f32[128,512]{1,0:T(8,128)S(1)} %multiply_add_fusion.7), channel_id=1, source_target_pairs={{4,0},{8,4},{12,8},{16,12},{20,16},{24,20},{28,24},{32,28},{36,32}... | collective-permute-start | bytes 786440 | tf_op jit(solution)/shard_map/while/body/eval_jaxpr/ppermute | solution.py:31
  550.5 9.8 %collective-permute-start = (f32[128,512]{1,0:T(8,128)S(1)}, f32[128,512]{1,0:T(8,128)S(1)}, u32[]{:S(2)}, u32[]{:S(2)}) collective-permute-start(f32[128,512]{1,0:T(8,128)S(1)} %multiply_add_fusion.7), channel_id=1, source_target_pairs={{4,0},{8,4},{12,8},{16,12},{20,16},{24,20},{28,24},{32,28},{36,32}... | collective-permute-start | bytes 786440 | tf_op jit(solution)/shard_map/while/body/eval_jaxpr/ppermute | solution.py:31
  (42 other events, 606.8 us)
Sparse Core Ops, SparseCore 0:
  19.0 32.8 reduce-scatter.1
  644.5 132.9 all-reduce.5
